TPU v7x, 32 devices: a whole 2x2x4 slice. The times are simulated.
32 devices in a mesh: brick: 4 (over z), batch: 8 (over y, x, core).
Axes of the slice: x: 2, y: 2, z: 4, core: 2. Of those that a mesh axis runs over, the one named last changes fastest.
Arguments:
- coarse: bfloat16 [8, 4, 4, 8, 1024], P('batch', 'brick'), may hold values from -6 to 6
- coarse_mask: int32 [8, 4, 256], P('batch', 'brick'), may hold values 0 or 1
- skip: bfloat16 [8, 4, 8, 16, 1024], P('batch', 'brick'), may hold values from -6 to 6
- fine_mask: int32 [8, 4, 2048], P('batch', 'brick'), may hold values 0 or 1
- up_weight: bfloat16 [27, 64, 128], replicated, may hold values from -0.25 to 0.25
- fine_grad: bfloat16 [8, 4, 8, 16, 1024], P('batch', 'brick'), may hold values from -6 to 6
Outputs:
- fine_out: bfloat16 [8, 4, 8, 16, 1024], P('batch', 'brick')
- coarse_grad: bfloat16 [8, 4, 4, 8, 1024], P('batch', 'brick')
- weight_grad: float32 [27, 64, 128], replicated
All inputs are finite; a program needn't handle non-finite values. No bound on the sum of `coarse_mask` or of `fine_mask` on one device may be relied on, other than what follows from the above.
Results may differ from a plain program's by a relative error of at most 0.0035.
Values may be sent and summed in bfloat16 or wider, within the bound.
No kernel may reach another device: no remote copies, remote signals or barrier semaphores. Data moves between devices by JAX's collectives and lax.ppermute only.
A program may use at most 64 MiB of HBM per device.

v0:
```python
import math
import jax
import jax.numpy as jnp
from jax import lax
from jax.sharding import PartitionSpec as P

EVEN_TAPS = ((1, 0),)
ODD_TAPS = ((2, 0), (0, 1))
DIRECTIONS = ((1, 0, 0), (0, 1, 0), (0, 0, 1), (1, 1, 0), (1, 0, 1), (0, 1, 1), (1, 1, 1))
STRIDES = (4, 2, 1)


def from_behind(shard, axis, by):
    size = lax.axis_size(axis)
    pairs = [(i, i + by) for i in range(size) if 0 <= i + by < size]
    return lax.ppermute(shard, axis, pairs)


def tap_pairs(parity):
    if parity == 0:
        return EVEN_TAPS
    return ODD_TAPS


def spread(padded, weight):
    counts = (padded.shape[0] - 1, padded.shape[1] - 1, padded.shape[2] - 1)
    outputs = weight.shape[1]
    parts = []
    for parity_x in range(2):
        for parity_y in range(2):
            for parity_z in range(2):
                total = jnp.zeros(counts + (outputs,), jnp.float32)
                for tap_x, start_x in tap_pairs(parity_x):
                    for tap_y, start_y in tap_pairs(parity_y):
                        for tap_z, start_z in tap_pairs(parity_z):
                            window = padded[
                                start_x : start_x + counts[0],
                                start_y : start_y + counts[1],
                                start_z : start_z + counts[2],
                            ]
                            total = total + jnp.einsum(
                                "abci,oi->abco",
                                window,
                                weight[9 * tap_x + 3 * tap_y + tap_z],
                                preferred_element_type=jnp.float32,
                            )
                parts.append(total)
    stacked = jnp.stack(parts).reshape((2, 2, 2) + counts + (outputs,))
    return stacked.transpose(3, 0, 4, 1, 5, 2, 6).reshape(
        2 * counts[0], 2 * counts[1], 2 * counts[2], outputs
    )


def pick(field, tap, count, axis):
    return lax.slice_in_dim(field, tap, tap + 2 * count - 1, 2, axis)


def adjoint(widened, masked, weight):
    counts = masked.shape[:3]
    back = jnp.zeros(masked.shape, jnp.float32)
    grads = []
    for tap_x in range(3):
        along_x = pick(widened, tap_x, counts[0], 0)
        for tap_y in range(3):
            along_y = pick(along_x, tap_y, counts[1], 1)
            for tap_z in range(3):
                chosen = pick(along_y, tap_z, counts[2], 2)
                index = 9 * tap_x + 3 * tap_y + tap_z
                back = back + jnp.einsum(
                    "abco,oi->abci", chosen, weight[index], preferred_element_type=jnp.float32
                )
                grads.append(
                    jnp.einsum("abco,abci->oi", chosen, masked, preferred_element_type=jnp.float32)
                )
    return (back, jnp.stack(grads))


def offset(direction):
    return 4 * direction[0] + 2 * direction[1] + direction[2]


def allowed(direction, grid_y, grid_z, side):
    result = grid_y >= 0
    if direction[1]:
        result = result & (grid_y == side)
    if direction[2]:
        result = result & (grid_z == side)
    return result


def flatten(piece):
    return piece.reshape(piece.shape[0], -1)


def segment_index(other, axis, edge):
    if other < axis:
        return slice(1, None)
    if other > axis:
        return slice(None)
    return edge


def unit_of(axis):
    return tuple((1 if other == axis else 0 for other in range(3)))


def body(coarse, coarse_mask, skip, fine_mask, up_weight, fine_grad):
    rank = lax.axis_index("brick")
    grid_y = rank // 2 % 2
    grid_z = rank % 2
    size_x, size_y, merged = coarse.shape[2:]
    channels_out = up_weight.shape[1]
    channels_in = up_weight.shape[2]
    size_z = merged // channels_in
    fine_x, fine_y, fine_merged = skip.shape[2:]
    fine_z = fine_merged // channels_out
    coarse_keep = coarse_mask.reshape(size_x, size_y, size_z, 1).astype(jnp.bfloat16)
    masked = coarse.reshape(size_x, size_y, size_z, channels_in) * coarse_keep
    extended = spread(jnp.pad(masked, ((1, 1), (1, 1), (1, 1), (0, 0))), up_weight)[1:, 1:, 1:]
    for axis in range(3):
        source = tuple((segment_index(other, axis, slice(0, 1)) for other in range(3)))
        piece = extended[source]
        got = from_behind(flatten(piece).astype(jnp.bfloat16), "brick", -STRIDES[axis]).astype(
            jnp.float32
        )
        got = jnp.where(allowed(unit_of(axis), grid_y, grid_z, 0), got, 0.0).reshape(piece.shape)
        target = tuple((segment_index(other, axis, slice(-1, None)) for other in range(3)))
        extended = extended.at[target].add(got)
    up = extended[1:, 1:, 1:]
    fine_keep = fine_mask.reshape(fine_x, fine_y, fine_z, 1)
    fine = fine_keep.astype(jnp.float32) * (
        skip.reshape(fine_x, fine_y, fine_z, channels_out).astype(jnp.float32) + up
    )
    fine_out = fine.astype(jnp.bfloat16).reshape(skip.shape)
    cotangent = fine_grad.reshape(fine_x, fine_y, fine_z, channels_out) * fine_keep.astype(
        jnp.bfloat16
    )
    widened = jnp.pad(cotangent, ((1, 0), (1, 0), (1, 0), (0, 0)))
    for direction in DIRECTIONS:
        source = tuple((slice(-1, None) if flag else slice(None) for flag in direction))
        piece = cotangent[source]
        got = from_behind(flatten(piece), "brick", offset(direction))
        got = jnp.where(allowed(direction, grid_y, grid_z, 1), got, 0.0).reshape(piece.shape)
        target = tuple((slice(0, 1) if flag else slice(1, None) for flag in direction))
        widened = widened.at[target].set(got)
    back, grads = adjoint(widened, masked, up_weight)
    coarse_grad = (
        (back * coarse_keep.astype(jnp.float32)).astype(jnp.bfloat16).reshape(coarse.shape)
    )
    summed = lax.psum(grads, ("brick", "batch"))
    scale = 1.0 / math.sqrt(
        lax.axis_size("brick") * lax.axis_size("batch") * size_x * size_y * size_z
    )
    return (fine_out, coarse_grad, summed * scale)


def solution(mesh):
    in_specs = (
        P("batch", "brick", None, None, None),
        P("batch", "brick", None),
        P("batch", "brick", None, None, None),
        P("batch", "brick", None),
        P(),
        P("batch", "brick", None, None, None),
    )
    out_specs = (P("batch", "brick", None, None, None), P("batch", "brick", None, None, None), P())
    return jax.shard_map(body, mesh=mesh, in_specs=in_specs, out_specs=out_specs, check_vma=False)
```

profile of v0, /device:TPU:0, one launch (start us, length us, event | category | flops | bytes accessed | tf_op | source)
XLA Modules:
  0.0 260.1 jit_solution(2375744965565836065)
XLA Ops:
  7.2 1.4 reshape.523
  11.3 5.9 %collective-permute-start.4 = (bf16[8,1024]{1,0:T(8,128)(2,1)S(1)}, bf16[8,1024]{1,0:T(8,128)(2,1)S(1)}, u32[]{:S(2)}, u32[]{:S(2)}) collective-permute-start(bf16[8,1024]{1,0:T(8,128)(2,1)S(1)} %reshape.526), channel_id=1, source_target_pairs={{0,16},{8,24},{1,17},{9,25},{2,18},{10,26},{3,19},{11,27},{4,20},{... | collective-permute-start | bytes 49160 | tf_op jit(solution)/shard_map/ppermute | solution.py:16
  17.6 3.5 %collective-permute-start.5 = (bf16[8,1024]{1,0:T(8,128)(2,1)S(1)}, bf16[8,1024]{1,0:T(8,128)(2,1)S(1)}, u32[]{:S(2)}, u32[]{:S(2)}) collective-permute-start(bf16[8,1024]{1,0:T(8,128)(2,1)S(1)} %reshape.528), channel_id=1, source_target_pairs={{0,8},{8,16},{16,24},{1,9},{9,17},{17,25},{2,10},{10,18},{18,26},{... | collective-permute-start | bytes 49160 | tf_op jit(solution)/shard_map/ppermute | solution.py:16
  31.6 2.0 copy.82
  33.7 2.4 reshape.518
  36.1 1.5 slice.770
  37.6 1.3 pad.47
  39.8 2.2 reshape.539
  42.7 1.3 collective-permute-start.8
  44.0 1.3 collective-permute-done.8
  46.0 1.3 collective-permute-start
  48.5 1.4 scatter.26
  50.5 1.1 fusion.189
  51.6 1.3 slice.733
  53.0 1.3 slice.734
  54.2 1.3 slice.735
  55.5 1.3 slice.737
  56.8 1.3 slice.738
  58.1 1.3 slice.739
  59.4 1.3 slice.741
  60.6 1.3 slice.742
  61.9 1.3 slice.743
  63.2 2.4 fusion.190
  65.6 2.8 %slice.746 = bf16[4,8,8,64]{3,2,1,0:T(8,128)(2,1)} slice(bf16[4,8,17,64]{3,2,1,0:T(8,128)(2,1)} %get-tuple-element.135), slice={[0:4:1], [0:8:1], [0:15:2], [0:64:1]} | slice | bytes 65536 | tf_op jit(solution)/shard_map/slice | solution.py:55
  68.4 2.8 %slice.747 = bf16[4,8,8,64]{3,2,1,0:T(8,128)(2,1)} slice(bf16[4,8,17,64]{3,2,1,0:T(8,128)(2,1)} %get-tuple-element.135), slice={[0:4:1], [0:8:1], [1:16:2], [0:64:1]} | slice | bytes 65536 | tf_op jit(solution)/shard_map/slice | solution.py:55
  71.1 2.8 %slice.748 = bf16[4,8,8,64]{3,2,1,0:T(8,128)(2,1)} slice(bf16[4,8,17,64]{3,2,1,0:T(8,128)(2,1)} %get-tuple-element.135), slice={[0:4:1], [0:8:1], [2:17:2], [0:64:1]} | slice | bytes 65536 | tf_op jit(solution)/shard_map/slice | solution.py:55
  74.0 2.8 %slice.750 = bf16[4,8,8,64]{3,2,1,0:T(8,128)(2,1)} slice(bf16[4,8,17,64]{3,2,1,0:T(8,128)(2,1)} %get-tuple-element.136), slice={[0:4:1], [0:8:1], [0:15:2], [0:64:1]} | slice | bytes 65536 | tf_op jit(solution)/shard_map/slice | solution.py:55
  76.7 2.7 %slice.751 = bf16[4,8,8,64]{3,2,1,0:T(8,128)(2,1)} slice(bf16[4,8,17,64]{3,2,1,0:T(8,128)(2,1)} %get-tuple-element.136), slice={[0:4:1], [0:8:1], [1:16:2], [0:64:1]} | slice | bytes 65536 | tf_op jit(solution)/shard_map/slice | solution.py:55
  79.5 2.8 %slice.752 = bf16[4,8,8,64]{3,2,1,0:T(8,128)(2,1)} slice(bf16[4,8,17,64]{3,2,1,0:T(8,128)(2,1)} %get-tuple-element.136), slice={[0:4:1], [0:8:1], [2:17:2], [0:64:1]} | slice | bytes 65536 | tf_op jit(solution)/shard_map/slice | solution.py:55
  82.3 1.3 slice.754
  83.6 1.3 slice.755
  84.9 1.3 slice.756
  86.1 1.3 slice.759
  87.4 1.3 slice.760
  88.7 1.3 slice.761
  91.1 1.7 fusion.43
  92.9 1.0 fusion.110
  93.9 1.7 fusion.42
  95.6 1.7 fusion.41
  97.3 1.7 fusion.40
  98.9 1.7 fusion.39
  104.7 1.7 fusion.33
  106.4 1.7 fusion.32
  120.4 1.0 convolution_add_fusion.44
  121.4 1.0 convolution_add_fusion.43
  122.5 1.0 convolution_add_fusion.42
  123.5 1.0 convolution_add_fusion.41
  126.9 1.0 convolution_add_fusion.35
  127.9 1.0 convolution_add_fusion.34
  136.7 1.5 convolution_add_fusion.21
  138.3 1.7 fusion.48
  142.7 1.3 collective-permute-start.1
  144.0 1.1 convolution_add_fusion.20
  145.1 4.1 %collective-permute-done.1 = bf16[8,1088]{1,0:T(8,128)(2,1)S(1)} collective-permute-done((bf16[8,1088]{1,0:T(8,128)(2,1)S(1)}, bf16[8,1088]{1,0:T(8,128)(2,1)S(1)}, u32[]{:S(2)}, u32[]{:S(2)}) %collective-permute-start.1) | collective-permute-done | bytes 17440 | tf_op jit(solution)/shard_map/ppermute | solution.py:16
  149.3 1.6 fusion.47
  150.9 1.2 fusion.50
  152.2 1.3 collective-permute-start.2
  155.1 2.8 %collective-permute-done.2 = bf16[8,1024]{1,0:T(8,128)(2,1)S(1)} collective-permute-done((bf16[8,1024]{1,0:T(8,128)(2,1)S(1)}, bf16[8,1024]{1,0:T(8,128)(2,1)S(1)}, u32[]{:S(2)}, u32[]{:S(2)}) %collective-permute-start.2) | collective-permute-done | bytes 16416 | tf_op jit(solution)/shard_map/ppermute | solution.py:16
  158.0 1.1 slice_add_fusion.3
  159.1 3.0 %scatter-add.14 = f32[9,17,17,64]{3,2,1,0:T(8,128)} dynamic-update-slice(f32[9,17,17,64]{3,2,1,0:T(8,128)} %fusion.47, f32[8,16,1,64]{3,2,1,0:T(1,128)S(1)} %slice_add_fusion.3, s32[]{:T(128)} %constant.355.clone.1, s32[]{:T(128)} %constant.355.clone.1, s32[]{:T(128)} %constant.361.clone.1, s32[]{:T(128)} %constant.356.clone.1) | dynamic-update-slice | bytes 65540 | tf_op jit(solution)/shard_map/scatter-add | solution.py:128
  162.1 1.7 fusion.45
  163.8 1.1 reshape.522
  164.9 86.2 %all-reduce.4.cloned.1.call-done = f32[27,64,128]{2,1,0:T(8,128)} async-done(((f32[27,64,128]{2,1,0:T(8,128)}), f32[27,64,128]{2,1,0:T(8,128)}) %all-reduce.4.cloned.1.call-update) | async-done | bytes 884752 | tf_op jit(solution)/shard_map/psum | solution.py:150
  251.1 2.2 broadcast_multiply_fusion
  (208 shorter events, 49.5 us)
Async XLA Ops:
  7.2 18.2 %copy-start.2 = (bf16[27,64,128]{2,1,0:T(8,128)(2,1)S(1)}, bf16[27,64,128]{2,1,0:T(8,128)(2,1)}, u32[]{:S(2)}) copy-start(bf16[27,64,128]{2,1,0:T(8,128)(2,1)} %param.30) | copy-start | bytes 1327108
  7.2 243.9 %all-reduce.4.cloned.1.call-start = ((), (), s32[]{:S(2)}) async-start(), calls=%async_computation | async-start | bytes 1769472 | tf_op jit(solution)/shard_map/psum | solution.py:150
  9.8 17.7 %copy-start.1 = (bf16[8,16,16,64]{3,2,1,0:T(8,128)(2,1)}, bf16[8,16,16,64]{3,2,1,0:T(8,128)(2,1)S(1)}, u32[]{:S(2)}) copy-start(bf16[8,16,16,64]{3,2,1,0:T(8,128)(2,1)S(1)} %broadcast_multiply_fusion.1) | copy-start | bytes 786436
  10.6 37.2 %collective-permute-start.3 = (bf16[1,16384]{1,0:T(2,128)(2,1)}, bf16[1,16384]{1,0:T(2,128)(2,1)S(1)}, u32[]{:S(2)}, u32[]{:S(2)}) collective-permute-start(bf16[1,16384]{1,0:T(2,128)(2,1)} %reshape.524), channel_id=1, source_target_pairs={} | collective-permute-start | bytes 98312 | tf_op jit(solution)/shard_map/ppermute | solution.py:16
  11.3 36.1 %collective-permute-start.4 = (bf16[8,1024]{1,0:T(8,128)(2,1)S(1)}, bf16[8,1024]{1,0:T(8,128)(2,1)S(1)}, u32[]{:S(2)}, u32[]{:S(2)}) collective-permute-start(bf16[8,1024]{1,0:T(8,128)(2,1)S(1)} %reshape.526), channel_id=1, source_target_pairs={{0,16},{8,24},{1,17},{9,25},{2,18},{10,26},{3,19},{11,27},{4,20},{... | collective-permute-start | bytes 49160 | tf_op jit(solution)/shard_map/ppermute | solution.py:16
  17.6 29.9 %collective-permute-start.5 = (bf16[8,1024]{1,0:T(8,128)(2,1)S(1)}, bf16[8,1024]{1,0:T(8,128)(2,1)S(1)}, u32[]{:S(2)}, u32[]{:S(2)}) collective-permute-start(bf16[8,1024]{1,0:T(8,128)(2,1)S(1)} %reshape.528), channel_id=1, source_target_pairs={{0,8},{8,16},{16,24},{1,9},{9,17},{17,25},{2,10},{10,18},{18,26},{... | collective-permute-start | bytes 49160 | tf_op jit(solution)/shard_map/ppermute | solution.py:16
  21.2 24.8 %collective-permute-start.6 = (bf16[1,1024]{1,0:T(2,128)(2,1)S(1)}, bf16[1,1024]{1,0:T(2,128)(2,1)S(1)}, u32[]{:S(2)}, u32[]{:S(2)}) collective-permute-start(bf16[1,1024]{1,0:T(2,128)(2,1)S(1)} %reshape.530), channel_id=1, source_target_pairs={} | collective-permute-start | bytes 6152 | tf_op jit(solution)/shard_map/ppermute | solution.py:16
  21.9 20.8 %collective-permute-start.9 = (bf16[1,64]{1,0:T(2,128)(2,1)S(1)}, bf16[1,64]{1,0:T(2,128)(2,1)S(1)}, u32[]{:S(2)}, u32[]{:S(2)}) collective-permute-start(bf16[1,64]{1,0:T(2,128)(2,1)S(1)} %slice_bitcast_fusion), channel_id=1, source_target_pairs={} | collective-permute-start | bytes 392 | tf_op jit(solution)/shard_map/ppermute | solution.py:16
  36.1 1.5 copy-start.34
  42.7 2.6 collective-permute-start.8
  45.3 2.0 collective-permute-start.7
  46.0 92.3 %collective-permute-start = (bf16[1,18496]{1,0:T(2,128)(2,1)}, bf16[1,18496]{1,0:T(2,128)(2,1)}, u32[]{:S(2)}, u32[]{:S(2)}) collective-permute-start(bf16[1,18496]{1,0:T(2,128)(2,1)} %convert_element_type.107), channel_id=1, source_target_pairs={} | collective-permute-start | bytes 110984 | tf_op jit(solution)/shard_map/ppermute | solution.py:16
  56.8 36.1 %copy-start.3 = (bf16[27,64,128]{2,1,0:T(8,128)(2,1)S(1)}, bf16[27,64,128]{2,1,0:T(8,128)(2,1)}, u32[]{:S(2)}) copy-start(bf16[27,64,128]{2,1,0:T(8,128)(2,1)} %param.30) | copy-start | bytes 1327108
  90.0 10.6 %copy-start.29 = (bf16[4,8,8,64]{3,2,1,0:T(8,128)(2,1)S(1)}, bf16[4,8,8,64]{3,2,1,0:T(8,128)(2,1)}, u32[]{:S(2)}) copy-start(bf16[4,8,8,64]{3,2,1,0:T(8,128)(2,1)} %slice.739) | copy-start | bytes 98308
  90.2 25.3 %copy-start.7 = (bf16[4,8,8,64]{3,2,1,0:T(8,128)(2,1)}, bf16[4,8,8,64]{3,2,1,0:T(8,128)(2,1)S(1)}, u32[]{:S(2)}) copy-start(bf16[4,8,8,64]{3,2,1,0:T(8,128)(2,1)S(1)} %slice.763) | copy-start | bytes 98308
  90.5 10.9 %copy-start.31 = (bf16[4,8,8,64]{3,2,1,0:T(8,128)(2,1)S(1)}, bf16[4,8,8,64]{3,2,1,0:T(8,128)(2,1)}, u32[]{:S(2)}) copy-start(bf16[4,8,8,64]{3,2,1,0:T(8,128)(2,1)} %slice.741) | copy-start | bytes 98308
  90.9 27.8 %copy-start.6 = (bf16[4,8,8,64]{3,2,1,0:T(8,128)(2,1)}, bf16[4,8,8,64]{3,2,1,0:T(8,128)(2,1)S(1)}, u32[]{:S(2)}) copy-start(bf16[4,8,8,64]{3,2,1,0:T(8,128)(2,1)S(1)} %slice.768) | copy-start | bytes 98308
  91.1 28.4 %copy-start.4 = (bf16[4,8,8,64]{3,2,1,0:T(8,128)(2,1)}, bf16[4,8,8,64]{3,2,1,0:T(8,128)(2,1)S(1)}, u32[]{:S(2)}) copy-start(bf16[4,8,8,64]{3,2,1,0:T(8,128)(2,1)S(1)} %slice.769) | copy-start | bytes 98308
  91.1 11.2 %copy-start.25 = (bf16[4,8,8,64]{3,2,1,0:T(8,128)(2,1)S(1)}, bf16[4,8,8,64]{3,2,1,0:T(8,128)(2,1)}, u32[]{:S(2)}) copy-start(bf16[4,8,8,64]{3,2,1,0:T(8,128)(2,1)} %slice.742) | copy-start | bytes 98308
  91.1 12.0 %copy-start.21 = (bf16[4,8,8,64]{3,2,1,0:T(8,128)(2,1)S(1)}, bf16[4,8,8,64]{3,2,1,0:T(8,128)(2,1)}, u32[]{:S(2)}) copy-start(bf16[4,8,8,64]{3,2,1,0:T(8,128)(2,1)} %slice.743) | copy-start | bytes 98308
  91.1 12.8 %copy-start.33 = (bf16[4,8,8,64]{3,2,1,0:T(8,128)(2,1)S(1)}, bf16[4,8,8,64]{3,2,1,0:T(8,128)(2,1)}, u32[]{:S(2)}) copy-start(bf16[4,8,8,64]{3,2,1,0:T(8,128)(2,1)} %slice.746) | copy-start | bytes 98308
  91.1 16.9 %copy-start.32 = (bf16[4,8,8,64]{3,2,1,0:T(8,128)(2,1)S(1)}, bf16[4,8,8,64]{3,2,1,0:T(8,128)(2,1)}, u32[]{:S(2)}) copy-start(bf16[4,8,8,64]{3,2,1,0:T(8,128)(2,1)} %slice.750) | copy-start | bytes 98308
  92.9 16.0 %copy-start.27 = (bf16[4,8,8,64]{3,2,1,0:T(8,128)(2,1)S(1)}, bf16[4,8,8,64]{3,2,1,0:T(8,128)(2,1)}, u32[]{:S(2)}) copy-start(bf16[4,8,8,64]{3,2,1,0:T(8,128)(2,1)} %slice.751) | copy-start | bytes 98308
  95.6 14.1 %copy-start.23 = (bf16[4,8,8,64]{3,2,1,0:T(8,128)(2,1)S(1)}, bf16[4,8,8,64]{3,2,1,0:T(8,128)(2,1)}, u32[]{:S(2)}) copy-start(bf16[4,8,8,64]{3,2,1,0:T(8,128)(2,1)} %slice.752) | copy-start | bytes 98308
  97.3 13.3 %copy-start.19 = (bf16[4,8,8,64]{3,2,1,0:T(8,128)(2,1)S(1)}, bf16[4,8,8,64]{3,2,1,0:T(8,128)(2,1)}, u32[]{:S(2)}) copy-start(bf16[4,8,8,64]{3,2,1,0:T(8,128)(2,1)} %slice.754) | copy-start | bytes 98308
  98.9 12.4 %copy-start.17 = (bf16[4,8,8,64]{3,2,1,0:T(8,128)(2,1)S(1)}, bf16[4,8,8,64]{3,2,1,0:T(8,128)(2,1)}, u32[]{:S(2)}) copy-start(bf16[4,8,8,64]{3,2,1,0:T(8,128)(2,1)} %slice.755) | copy-start | bytes 98308
  100.6 11.5 %copy-start.15 = (bf16[4,8,8,64]{3,2,1,0:T(8,128)(2,1)S(1)}, bf16[4,8,8,64]{3,2,1,0:T(8,128)(2,1)}, u32[]{:S(2)}) copy-start(bf16[4,8,8,64]{3,2,1,0:T(8,128)(2,1)} %slice.756) | copy-start | bytes 98308
  101.5 11.5 %copy-start.13 = (bf16[4,8,8,64]{3,2,1,0:T(8,128)(2,1)S(1)}, bf16[4,8,8,64]{3,2,1,0:T(8,128)(2,1)}, u32[]{:S(2)}) copy-start(bf16[4,8,8,64]{3,2,1,0:T(8,128)(2,1)} %slice.759) | copy-start | bytes 98308
  102.3 11.5 %copy-start.11 = (bf16[4,8,8,64]{3,2,1,0:T(8,128)(2,1)S(1)}, bf16[4,8,8,64]{3,2,1,0:T(8,128)(2,1)}, u32[]{:S(2)}) copy-start(bf16[4,8,8,64]{3,2,1,0:T(8,128)(2,1)} %slice.760) | copy-start | bytes 98308
  103.1 11.5 %copy-start.9 = (bf16[4,8,8,64]{3,2,1,0:T(8,128)(2,1)S(1)}, bf16[4,8,8,64]{3,2,1,0:T(8,128)(2,1)}, u32[]{:S(2)}) copy-start(bf16[4,8,8,64]{3,2,1,0:T(8,128)(2,1)} %slice.761) | copy-start | bytes 98308
  113.8 10.7 %copy-start.30 = (bf16[4,8,8,64]{3,2,1,0:T(8,128)(2,1)S(1)}, bf16[4,8,8,64]{3,2,1,0:T(8,128)(2,1)}, u32[]{:S(2)}) copy-start(bf16[4,8,8,64]{3,2,1,0:T(8,128)(2,1)} %slice.739) | copy-start | bytes 98308
  115.4 10.2 %copy-start.26 = (bf16[4,8,8,64]{3,2,1,0:T(8,128)(2,1)S(1)}, bf16[4,8,8,64]{3,2,1,0:T(8,128)(2,1)}, u32[]{:S(2)}) copy-start(bf16[4,8,8,64]{3,2,1,0:T(8,128)(2,1)} %slice.742) | copy-start | bytes 98308
  116.2 9.6 %copy-start.22 = (bf16[4,8,8,64]{3,2,1,0:T(8,128)(2,1)S(1)}, bf16[4,8,8,64]{3,2,1,0:T(8,128)(2,1)}, u32[]{:S(2)}) copy-start(bf16[4,8,8,64]{3,2,1,0:T(8,128)(2,1)} %slice.743) | copy-start | bytes 98308
  118.7 11.2 %copy-start.28 = (bf16[4,8,8,64]{3,2,1,0:T(8,128)(2,1)S(1)}, bf16[4,8,8,64]{3,2,1,0:T(8,128)(2,1)}, u32[]{:S(2)}) copy-start(bf16[4,8,8,64]{3,2,1,0:T(8,128)(2,1)} %slice.751) | copy-start | bytes 98308
  119.5 10.6 %copy-start.24 = (bf16[4,8,8,64]{3,2,1,0:T(8,128)(2,1)S(1)}, bf16[4,8,8,64]{3,2,1,0:T(8,128)(2,1)}, u32[]{:S(2)}) copy-start(bf16[4,8,8,64]{3,2,1,0:T(8,128)(2,1)} %slice.752) | copy-start | bytes 98308
  120.3 9.9 %copy-start.20 = (bf16[4,8,8,64]{3,2,1,0:T(8,128)(2,1)S(1)}, bf16[4,8,8,64]{3,2,1,0:T(8,128)(2,1)}, u32[]{:S(2)}) copy-start(bf16[4,8,8,64]{3,2,1,0:T(8,128)(2,1)} %slice.754) | copy-start | bytes 98308
  120.3 10.1 %copy-start.18 = (bf16[4,8,8,64]{3,2,1,0:T(8,128)(2,1)S(1)}, bf16[4,8,8,64]{3,2,1,0:T(8,128)(2,1)}, u32[]{:S(2)}) copy-start(bf16[4,8,8,64]{3,2,1,0:T(8,128)(2,1)} %slice.755) | copy-start | bytes 98308
  120.4 10.2 %copy-start.16 = (bf16[4,8,8,64]{3,2,1,0:T(8,128)(2,1)S(1)}, bf16[4,8,8,64]{3,2,1,0:T(8,128)(2,1)}, u32[]{:S(2)}) copy-start(bf16[4,8,8,64]{3,2,1,0:T(8,128)(2,1)} %slice.756) | copy-start | bytes 98308
  120.4 11.2 %copy-start.14 = (bf16[4,8,8,64]{3,2,1,0:T(8,128)(2,1)S(1)}, bf16[4,8,8,64]{3,2,1,0:T(8,128)(2,1)}, u32[]{:S(2)}) copy-start(bf16[4,8,8,64]{3,2,1,0:T(8,128)(2,1)} %slice.759) | copy-start | bytes 98308
  121.4 11.0 %copy-start.12 = (bf16[4,8,8,64]{3,2,1,0:T(8,128)(2,1)S(1)}, bf16[4,8,8,64]{3,2,1,0:T(8,128)(2,1)}, u32[]{:S(2)}) copy-start(bf16[4,8,8,64]{3,2,1,0:T(8,128)(2,1)} %slice.760) | copy-start | bytes 98308
  122.5 10.8 %copy-start.10 = (bf16[4,8,8,64]{3,2,1,0:T(8,128)(2,1)S(1)}, bf16[4,8,8,64]{3,2,1,0:T(8,128)(2,1)}, u32[]{:S(2)}) copy-start(bf16[4,8,8,64]{3,2,1,0:T(8,128)(2,1)} %slice.761) | copy-start | bytes 98308
  123.5 10.7 %copy-start.8 = (bf16[4,8,8,64]{3,2,1,0:T(8,128)(2,1)S(1)}, bf16[4,8,8,64]{3,2,1,0:T(8,128)(2,1)}, u32[]{:S(2)}) copy-start(bf16[4,8,8,64]{3,2,1,0:T(8,128)(2,1)} %copy-done.7) | copy-start | bytes 98308
  130.1 23.4 %copy-start.5 = (bf16[4,8,8,64]{3,2,1,0:T(8,128)(2,1)S(1)}, bf16[4,8,8,64]{3,2,1,0:T(8,128)(2,1)}, u32[]{:S(2)}) copy-start(bf16[4,8,8,64]{3,2,1,0:T(8,128)(2,1)} %copy-done.4) | copy-start | bytes 98308
  130.6 31.5 %copy-start = (f32[8,16,16,64]{3,2,1,0:T(8,128)S(1)}, f32[8,16,16,64]{3,2,1,0:T(8,128)}, u32[]{:S(2)}) copy-start(f32[8,16,16,64]{3,2,1,0:T(8,128)} %reshape.539) | copy-start | bytes 1572868
  142.7 6.5 %collective-permute-start.1 = (bf16[8,1088]{1,0:T(8,128)(2,1)S(1)}, bf16[8,1088]{1,0:T(8,128)(2,1)S(1)}, u32[]{:S(2)}, u32[]{:S(2)}) collective-permute-start(bf16[8,1088]{1,0:T(8,128)(2,1)S(1)} %convert_element_type.109), channel_id=1, source_target_pairs={{16,0},{24,8},{17,1},{25,9},{18,2},{26,10},{19,3},{27,11},{20,4},{... | collective-permute-start | bytes 52232 | tf_op jit(solution)/shard_map/ppermute | solution.py:16
  152.2 5.6 %collective-permute-start.2 = (bf16[8,1024]{1,0:T(8,128)(2,1)S(1)}, bf16[8,1024]{1,0:T(8,128)(2,1)S(1)}, u32[]{:S(2)}, u32[]{:S(2)}) collective-permute-start(bf16[8,1024]{1,0:T(8,128)(2,1)S(1)} %convert_element_type.111), channel_id=1, source_target_pairs={{8,0},{16,8},{24,16},{9,1},{17,9},{25,17},{10,2},{18,10},{26,18},{... | collective-permute-start | bytes 49160 | tf_op jit(solution)/shard_map/ppermute | solution.py:16
Sparse Core Ops, SparseCore 0:
  120.5 130.5 all-reduce.3
where the time goes:
time: 263 us; the launch traced here: 260 us
  waiting for transfers between devices  94.5 us (36%)
  local copies, waits for them, and re-layouts  65.6 us (25%)
  matrix products  55.9 us (21%)
  starting transfers between devices  17.2 us (7%)
  between operations  14.9 us (6%)
  other arithmetic  12.1 us (5%)
    psum x1, waiting for transfers between devices, body(): summed = lax.psum(grads, ('brick', 'batch'))  86.2 us
    slice x30, local copies, waits for them, and re-layouts, pick(): return lax.slice_in_dim(field, tap, tap + 2 * count - 1, 2, axis)  40.5 us
    dot_general x27, matrix products, adjoint(): jnp.einsum('abco,abci->oi', chosen, masked, preferred_element_type=jnp.fl...  28.1 us
    dot_general x27, matrix products, adjoint(): jnp.einsum('abco,oi->abci', chosen, weight[index], preferred_element_type...  20.8 us
    ppermute x10, starting transfers between devices, from_behind(): return lax.ppermute(shard, axis, pairs)  17.2 us
    ppermute x10, waiting for transfers between devices, from_behind(): return lax.ppermute(shard, axis, pairs)  8.22 us
    dot_general x27, matrix products, spread(): jnp.einsum('abci,oi->abco', window, weight[9 * tap_x + 3 * tap_y + tap_z]...  7.06 us
  transfers between devices with their start and end apart: 11, of which 4 were waited for; matrix products, arithmetic and copies ran while one was open for 49% of the time, Pallas kernels for 0%

commit v1 on v0

--- a/solution.py
+++ b/solution.py
@@ -8,6 +8,7 @@
 ODD_TAPS = ((2, 0), (0, 1))
 DIRECTIONS = ((1, 0, 0), (0, 1, 0), (0, 0, 1), (1, 1, 0), (1, 0, 1), (0, 1, 1), (1, 1, 1))
 STRIDES = (4, 2, 1)
+rails_point = lambda unit: lax.psum(lax.psum(unit, axis_name="batch"), axis_name="brick")
 
 
 def from_behind(shard, axis, by):
@@ -147,7 +148,7 @@
     coarse_grad = (
         (back * coarse_keep.astype(jnp.float32)).astype(jnp.bfloat16).reshape(coarse.shape)
     )
-    summed = lax.psum(grads, ("brick", "batch"))
+    summed = rails_point(grads)
     scale = 1.0 / math.sqrt(
         lax.axis_size("brick") * lax.axis_size("batch") * size_x * size_y * size_z
     )

time: 263 us -> 243 us (0.924)
  waiting for transfers between devices: 94.5 us -> 69.9 us
    psum x1 -> x2, waiting for transfers between devices: 86.2 us -> 64.9 us  [the longest x1 39.5 us: lax.psum(lax.psum(unit, axis_name='batch'), axis_name='brick')]
    ppermute x10, waiting for transfers between devices: 8.22 us -> 4.93 us  [from_behind(): return lax.ppermute(shard, axis, pairs)]
  transfers between devices with their start and end apart: 11 -> 12, of which waited for: 4 -> 4; matrix products, arithmetic and copies ran while one was open for 49% -> 55% of each run, Pallas kernels for 0% -> 0%
where the time goes in v1:
time: 243 us; the launch traced here: 240 us
  waiting for transfers between devices  69.9 us (29%)
  local copies, waits for them, and re-layouts  67.5 us (28%)
  matrix products  57 us (23%)
  starting transfers between devices  17.8 us (7%)
  between operations  14.8 us (6%)
  other arithmetic  12.7 us (5%)
    slice x30, local copies, waits for them, and re-layouts, pick(): return lax.slice_in_dim(field, tap, tap + 2 * count - 1, 2, axis)  40.5 us
    psum x1, waiting for transfers between devices, lax.psum(lax.psum(unit, axis_name='batch'), axis_name='brick')  39.5 us
    dot_general x27, matrix products, adjoint(): jnp.einsum('abco,abci->oi', chosen, masked, preferred_element_type=jnp.fl...  28.1 us
    psum x1, waiting for transfers between devices, lax.psum(unit, axis_name='batch')  25.4 us
    dot_general x27, matrix products, adjoint(): jnp.einsum('abco,oi->abci', chosen, weight[index], preferred_element_type...  21.9 us
    ppermute x10, starting transfers between devices, from_behind(): return lax.ppermute(shard, axis, pairs)  17.7 us
    dot_general x27, matrix products, spread(): jnp.einsum('abci,oi->abco', window, weight[9 * tap_x + 3 * tap_y + tap_z]...  7.05 us
    ppermute x10, waiting for transfers between devices, from_behind(): return lax.ppermute(shard, axis, pairs)  4.93 us
  transfers between devices with their start and end apart: 12, of which 4 were waited for; matrix products, arithmetic and copies ran while one was open for 55% of the time, Pallas kernels for 0%

profile of v1, /device:TPU:0, one launch (start us, length us, event | category | flops | bytes accessed | tf_op | source)
XLA Modules:
  0.0 239.7 jit_solution(12851487949499828995)
XLA Ops:
  7.2 1.4 reshape.523
  10.7 5.9 %collective-permute-start.4 = (bf16[8,1024]{1,0:T(8,128)(2,1)S(1)}, bf16[8,1024]{1,0:T(8,128)(2,1)S(1)}, u32[]{:S(2)}, u32[]{:S(2)}) collective-permute-start(bf16[8,1024]{1,0:T(8,128)(2,1)S(1)} %reshape.526), channel_id=1, source_target_pairs={{0,16},{8,24},{1,17},{9,25},{2,18},{10,26},{3,19},{11,27},{4,20},{... | collective-permute-start | bytes 49160 | tf_op jit(solution)/shard_map/ppermute | solution.py:17
  16.9 3.5 %collective-permute-start.5 = (bf16[8,1024]{1,0:T(8,128)(2,1)S(1)}, bf16[8,1024]{1,0:T(8,128)(2,1)S(1)}, u32[]{:S(2)}, u32[]{:S(2)}) collective-permute-start(bf16[8,1024]{1,0:T(8,128)(2,1)S(1)} %reshape.528), channel_id=1, source_target_pairs={{0,8},{8,16},{16,24},{1,9},{9,17},{17,25},{2,10},{10,18},{18,26},{... | collective-permute-start | bytes 49160 | tf_op jit(solution)/shard_map/ppermute | solution.py:17
  21.7 1.2 collective-permute-start.9
  32.6 2.1 copy.82
  34.6 2.4 reshape.518
  37.0 1.5 slice.770
  38.5 1.3 pad.47
  40.7 2.2 reshape.539
  43.7 1.3 collective-permute-start.8
  47.5 1.3 collective-permute-start
  50.7 1.4 scatter.26
  54.4 1.1 fusion.189
  55.5 1.3 slice.733
  56.9 1.3 slice.734
  58.1 1.3 slice.735
  59.4 1.3 slice.737
  60.7 1.3 slice.738
  62.0 1.3 slice.739
  63.3 1.3 slice.741
  64.5 1.3 slice.742
  65.8 1.3 slice.743
  67.1 2.4 fusion.190
  69.5 2.8 %slice.746 = bf16[4,8,8,64]{3,2,1,0:T(8,128)(2,1)} slice(bf16[4,8,17,64]{3,2,1,0:T(8,128)(2,1)} %get-tuple-element.135), slice={[0:4:1], [0:8:1], [0:15:2], [0:64:1]} | slice | bytes 65536 | tf_op jit(solution)/shard_map/slice | solution.py:56
  72.2 2.8 %slice.747 = bf16[4,8,8,64]{3,2,1,0:T(8,128)(2,1)} slice(bf16[4,8,17,64]{3,2,1,0:T(8,128)(2,1)} %get-tuple-element.135), slice={[0:4:1], [0:8:1], [1:16:2], [0:64:1]} | slice | bytes 65536 | tf_op jit(solution)/shard_map/slice | solution.py:56
  75.0 2.8 %slice.748 = bf16[4,8,8,64]{3,2,1,0:T(8,128)(2,1)} slice(bf16[4,8,17,64]{3,2,1,0:T(8,128)(2,1)} %get-tuple-element.135), slice={[0:4:1], [0:8:1], [2:17:2], [0:64:1]} | slice | bytes 65536 | tf_op jit(solution)/shard_map/slice | solution.py:56
  77.8 2.8 %slice.750 = bf16[4,8,8,64]{3,2,1,0:T(8,128)(2,1)} slice(bf16[4,8,17,64]{3,2,1,0:T(8,128)(2,1)} %get-tuple-element.136), slice={[0:4:1], [0:8:1], [0:15:2], [0:64:1]} | slice | bytes 65536 | tf_op jit(solution)/shard_map/slice | solution.py:56
  80.6 2.8 %slice.751 = bf16[4,8,8,64]{3,2,1,0:T(8,128)(2,1)} slice(bf16[4,8,17,64]{3,2,1,0:T(8,128)(2,1)} %get-tuple-element.136), slice={[0:4:1], [0:8:1], [1:16:2], [0:64:1]} | slice | bytes 65536 | tf_op jit(solution)/shard_map/slice | solution.py:56
  83.4 2.8 %slice.752 = bf16[4,8,8,64]{3,2,1,0:T(8,128)(2,1)} slice(bf16[4,8,17,64]{3,2,1,0:T(8,128)(2,1)} %get-tuple-element.136), slice={[0:4:1], [0:8:1], [2:17:2], [0:64:1]} | slice | bytes 65536 | tf_op jit(solution)/shard_map/slice | solution.py:56
  86.2 1.3 slice.754
  87.5 1.3 slice.755
  88.8 1.3 slice.756
  90.1 1.3 slice.759
  91.3 1.3 slice.760
  92.6 1.3 slice.761
  95.0 1.7 fusion.43
  96.8 1.0 fusion.110
  97.8 1.7 fusion.42
  99.5 1.7 fusion.41
  101.1 1.7 fusion.40
  102.8 1.7 fusion.39
  108.6 1.7 fusion.33
  110.3 1.7 fusion.32
  125.3 1.0 convolution_add_fusion.43
  126.3 1.0 convolution_add_fusion.42
  128.3 1.0 convolution_add_fusion.40
  131.4 1.0 convolution_add_fusion.36
  135.4 1.0 convolution_add_fusion.32
  141.6 1.5 convolution_add_fusion.21
  143.1 1.1 fusion.48
  146.1 1.3 collective-permute-start.1
  147.4 1.1 convolution_add_fusion.20
  148.5 4.1 %collective-permute-done.1 = bf16[8,1088]{1,0:T(8,128)(2,1)S(1)} collective-permute-done((bf16[8,1088]{1,0:T(8,128)(2,1)S(1)}, bf16[8,1088]{1,0:T(8,128)(2,1)S(1)}, u32[]{:S(2)}, u32[]{:S(2)}) %collective-permute-start.1) | collective-permute-done | bytes 17440 | tf_op jit(solution)/shard_map/ppermute | solution.py:17
  152.7 1.5 fusion.47
  154.2 1.2 fusion.50
  155.6 1.3 collective-permute-start.2
  156.9 25.4 %all-reduce.5.cloned.1.call-done = f32[27,64,128]{2,1,0:T(8,128)} async-done(((f32[27,64,128]{2,1,0:T(8,128)}), f32[27,64,128]{2,1,0:T(8,128)}) %all-reduce.5.cloned.1.call-update) | async-done | bytes 884752 | tf_op jit(solution)/shard_map/psum | solution.py:11
  182.3 1.0 fusion.16
  184.1 1.1 slice_add_fusion.3
  185.2 2.9 %scatter-add.14 = f32[9,17,17,64]{3,2,1,0:T(8,128)} dynamic-update-slice(f32[9,17,17,64]{3,2,1,0:T(8,128)} %fusion.47, f32[8,16,1,64]{3,2,1,0:T(1,128)S(1)} %slice_add_fusion.3, s32[]{:T(128)} %constant.355.clone.1, s32[]{:T(128)} %constant.355.clone.1, s32[]{:T(128)} %constant.361.clone.1, s32[]{:T(128)} %constant.356.clone.1) | dynamic-update-slice | bytes 65540 | tf_op jit(solution)/shard_map/scatter-add | solution.py:129
  188.2 1.9 fusion.45
  190.1 1.1 reshape.522
  191.1 39.5 %all-reduce.7.cloned.1.call-done = f32[27,64,128]{2,1,0:T(8,128)} async-done(((f32[27,64,128]{2,1,0:T(8,128)}), f32[27,64,128]{2,1,0:T(8,128)}) %all-reduce.7.cloned.1.call-update) | async-done | bytes 884752 | tf_op jit(solution)/shard_map/psum | solution.py:11
  230.6 2.2 broadcast_multiply_fusion
  (197 shorter events, 53.9 us)
Async XLA Ops:
  7.2 19.1 %copy-start.2 = (bf16[27,64,128]{2,1,0:T(8,128)(2,1)S(1)}, bf16[27,64,128]{2,1,0:T(8,128)(2,1)}, u32[]{:S(2)}) copy-start(bf16[27,64,128]{2,1,0:T(8,128)(2,1)} %param.30) | copy-start | bytes 1327108
  7.2 175.1 %all-reduce.5.cloned.1.call-start = ((), (), s32[]{:S(2)}) async-start(), calls=%async_computation | async-start | bytes 1769472 | tf_op jit(solution)/shard_map/psum | solution.py:11
  9.8 18.6 %copy-start.1 = (bf16[8,16,16,64]{3,2,1,0:T(8,128)(2,1)}, bf16[8,16,16,64]{3,2,1,0:T(8,128)(2,1)S(1)}, u32[]{:S(2)}) copy-start(bf16[8,16,16,64]{3,2,1,0:T(8,128)(2,1)S(1)} %broadcast_multiply_fusion.1) | copy-start | bytes 786436
  9.9 40.0 %collective-permute-start.3 = (bf16[1,16384]{1,0:T(2,128)(2,1)S(1)}, bf16[1,16384]{1,0:T(2,128)(2,1)S(1)}, u32[]{:S(2)}, u32[]{:S(2)}) collective-permute-start(bf16[1,16384]{1,0:T(2,128)(2,1)S(1)} %reshape.524), channel_id=1, source_target_pairs={} | collective-permute-start | bytes 98312 | tf_op jit(solution)/shard_map/ppermute | solution.py:17
  10.7 38.9 %collective-permute-start.4 = (bf16[8,1024]{1,0:T(8,128)(2,1)S(1)}, bf16[8,1024]{1,0:T(8,128)(2,1)S(1)}, u32[]{:S(2)}, u32[]{:S(2)}) collective-permute-start(bf16[8,1024]{1,0:T(8,128)(2,1)S(1)} %reshape.526), channel_id=1, source_target_pairs={{0,16},{8,24},{1,17},{9,25},{2,18},{10,26},{3,19},{11,27},{4,20},{... | collective-permute-start | bytes 49160 | tf_op jit(solution)/shard_map/ppermute | solution.py:17
  16.9 32.7 %collective-permute-start.5 = (bf16[8,1024]{1,0:T(8,128)(2,1)S(1)}, bf16[8,1024]{1,0:T(8,128)(2,1)S(1)}, u32[]{:S(2)}, u32[]{:S(2)}) collective-permute-start(bf16[8,1024]{1,0:T(8,128)(2,1)S(1)} %reshape.528), channel_id=1, source_target_pairs={{0,8},{8,16},{16,24},{1,9},{9,17},{17,25},{2,10},{10,18},{18,26},{... | collective-permute-start | bytes 49160 | tf_op jit(solution)/shard_map/ppermute | solution.py:17
  20.5 27.0 %collective-permute-start.6 = (bf16[1,1024]{1,0:T(2,128)(2,1)S(1)}, bf16[1,1024]{1,0:T(2,128)(2,1)S(1)}, u32[]{:S(2)}, u32[]{:S(2)}) collective-permute-start(bf16[1,1024]{1,0:T(2,128)(2,1)S(1)} %reshape.530), channel_id=1, source_target_pairs={} | collective-permute-start | bytes 6152 | tf_op jit(solution)/shard_map/ppermute | solution.py:17
  21.7 22.0 %collective-permute-start.9 = (bf16[1,64]{1,0:T(2,128)(2,1)}, bf16[1,64]{1,0:T(2,128)(2,1)}, u32[]{:S(2)}, u32[]{:S(2)}) collective-permute-start(bf16[1,64]{1,0:T(2,128)(2,1)} %slice_bitcast_fusion), channel_id=1, source_target_pairs={} | collective-permute-start | bytes 392 | tf_op jit(solution)/shard_map/ppermute | solution.py:17
  37.0 1.5 copy-start.27
  43.7 2.6 %collective-permute-start.8 = (bf16[8,64]{1,0:T(8,128)(2,1)S(1)}, bf16[8,64]{1,0:T(8,128)(2,1)S(1)}, u32[]{:S(2)}, u32[]{:S(2)}) collective-permute-start(bf16[8,64]{1,0:T(8,128)(2,1)S(1)} %bitcast.612), channel_id=1, source_target_pairs={{0,24},{1,25},{2,26},{3,27},{4,28},{5,29},{6,30},{7,31}} | collective-permute-start | bytes 3080 | tf_op jit(solution)/shard_map/ppermute | solution.py:17
  46.2 2.6 %collective-permute-start.7 = (bf16[1,1024]{1,0:T(2,128)(2,1)S(1)}, bf16[1,1024]{1,0:T(2,128)(2,1)S(1)}, u32[]{:S(2)}, u32[]{:S(2)}) collective-permute-start(bf16[1,1024]{1,0:T(2,128)(2,1)S(1)} %reshape.532), channel_id=1, source_target_pairs={} | collective-permute-start | bytes 6152 | tf_op jit(solution)/shard_map/ppermute | solution.py:17
  47.5 95.6 %collective-permute-start = (bf16[1,18496]{1,0:T(2,128)(2,1)}, bf16[1,18496]{1,0:T(2,128)(2,1)}, u32[]{:S(2)}, u32[]{:S(2)}) collective-permute-start(bf16[1,18496]{1,0:T(2,128)(2,1)} %convert_element_type.107), channel_id=1, source_target_pairs={} | collective-permute-start | bytes 110984 | tf_op jit(solution)/shard_map/ppermute | solution.py:17
  60.7 36.1 %copy-start.3 = (bf16[27,64,128]{2,1,0:T(8,128)(2,1)S(1)}, bf16[27,64,128]{2,1,0:T(8,128)(2,1)}, u32[]{:S(2)}) copy-start(bf16[27,64,128]{2,1,0:T(8,128)(2,1)} %param.30) | copy-start | bytes 1327108
  93.9 10.6 %copy-start.22 = (bf16[4,8,8,64]{3,2,1,0:T(8,128)(2,1)S(1)}, bf16[4,8,8,64]{3,2,1,0:T(8,128)(2,1)}, u32[]{:S(2)}) copy-start(bf16[4,8,8,64]{3,2,1,0:T(8,128)(2,1)} %slice.739) | copy-start | bytes 98308
  94.4 10.9 %copy-start.23 = (bf16[4,8,8,64]{3,2,1,0:T(8,128)(2,1)S(1)}, bf16[4,8,8,64]{3,2,1,0:T(8,128)(2,1)}, u32[]{:S(2)}) copy-start(bf16[4,8,8,64]{3,2,1,0:T(8,128)(2,1)} %slice.741) | copy-start | bytes 98308
  94.8 27.8 %copy-start.5 = (bf16[4,8,8,64]{3,2,1,0:T(8,128)(2,1)}, bf16[4,8,8,64]{3,2,1,0:T(8,128)(2,1)S(1)}, u32[]{:S(2)}) copy-start(bf16[4,8,8,64]{3,2,1,0:T(8,128)(2,1)S(1)} %slice.768) | copy-start | bytes 98308
  95.0 28.4 %copy-start.4 = (bf16[4,8,8,64]{3,2,1,0:T(8,128)(2,1)}, bf16[4,8,8,64]{3,2,1,0:T(8,128)(2,1)S(1)}, u32[]{:S(2)}) copy-start(bf16[4,8,8,64]{3,2,1,0:T(8,128)(2,1)S(1)} %slice.769) | copy-start | bytes 98308
  95.0 11.2 %copy-start.20 = (bf16[4,8,8,64]{3,2,1,0:T(8,128)(2,1)S(1)}, bf16[4,8,8,64]{3,2,1,0:T(8,128)(2,1)}, u32[]{:S(2)}) copy-start(bf16[4,8,8,64]{3,2,1,0:T(8,128)(2,1)} %slice.742) | copy-start | bytes 98308
  95.0 12.0 %copy-start.16 = (bf16[4,8,8,64]{3,2,1,0:T(8,128)(2,1)S(1)}, bf16[4,8,8,64]{3,2,1,0:T(8,128)(2,1)}, u32[]{:S(2)}) copy-start(bf16[4,8,8,64]{3,2,1,0:T(8,128)(2,1)} %slice.743) | copy-start | bytes 98308
  95.0 12.8 %copy-start.25 = (bf16[4,8,8,64]{3,2,1,0:T(8,128)(2,1)S(1)}, bf16[4,8,8,64]{3,2,1,0:T(8,128)(2,1)}, u32[]{:S(2)}) copy-start(bf16[4,8,8,64]{3,2,1,0:T(8,128)(2,1)} %slice.746) | copy-start | bytes 98308
  95.0 16.9 %copy-start.24 = (bf16[4,8,8,64]{3,2,1,0:T(8,128)(2,1)S(1)}, bf16[4,8,8,64]{3,2,1,0:T(8,128)(2,1)}, u32[]{:S(2)}) copy-start(bf16[4,8,8,64]{3,2,1,0:T(8,128)(2,1)} %slice.750) | copy-start | bytes 98308
  96.8 16.0 %copy-start.21 = (bf16[4,8,8,64]{3,2,1,0:T(8,128)(2,1)S(1)}, bf16[4,8,8,64]{3,2,1,0:T(8,128)(2,1)}, u32[]{:S(2)}) copy-start(bf16[4,8,8,64]{3,2,1,0:T(8,128)(2,1)} %slice.751) | copy-start | bytes 98308
  99.5 14.1 %copy-start.18 = (bf16[4,8,8,64]{3,2,1,0:T(8,128)(2,1)S(1)}, bf16[4,8,8,64]{3,2,1,0:T(8,128)(2,1)}, u32[]{:S(2)}) copy-start(bf16[4,8,8,64]{3,2,1,0:T(8,128)(2,1)} %slice.752) | copy-start | bytes 98308
  101.1 13.3 %copy-start.14 = (bf16[4,8,8,64]{3,2,1,0:T(8,128)(2,1)S(1)}, bf16[4,8,8,64]{3,2,1,0:T(8,128)(2,1)}, u32[]{:S(2)}) copy-start(bf16[4,8,8,64]{3,2,1,0:T(8,128)(2,1)} %slice.754) | copy-start | bytes 98308
  102.8 12.4 %copy-start.12 = (bf16[4,8,8,64]{3,2,1,0:T(8,128)(2,1)S(1)}, bf16[4,8,8,64]{3,2,1,0:T(8,128)(2,1)}, u32[]{:S(2)}) copy-start(bf16[4,8,8,64]{3,2,1,0:T(8,128)(2,1)} %slice.755) | copy-start | bytes 98308
  104.5 11.5 %copy-start.11 = (bf16[4,8,8,64]{3,2,1,0:T(8,128)(2,1)S(1)}, bf16[4,8,8,64]{3,2,1,0:T(8,128)(2,1)}, u32[]{:S(2)}) copy-start(bf16[4,8,8,64]{3,2,1,0:T(8,128)(2,1)} %slice.756) | copy-start | bytes 98308
  105.3 11.5 %copy-start.10 = (bf16[4,8,8,64]{3,2,1,0:T(8,128)(2,1)S(1)}, bf16[4,8,8,64]{3,2,1,0:T(8,128)(2,1)}, u32[]{:S(2)}) copy-start(bf16[4,8,8,64]{3,2,1,0:T(8,128)(2,1)} %slice.759) | copy-start | bytes 98308
  106.2 11.5 %copy-start.8 = (bf16[4,8,8,64]{3,2,1,0:T(8,128)(2,1)S(1)}, bf16[4,8,8,64]{3,2,1,0:T(8,128)(2,1)}, u32[]{:S(2)}) copy-start(bf16[4,8,8,64]{3,2,1,0:T(8,128)(2,1)} %slice.760) | copy-start | bytes 98308
  107.0 11.5 %copy-start.6 = (bf16[4,8,8,64]{3,2,1,0:T(8,128)(2,1)S(1)}, bf16[4,8,8,64]{3,2,1,0:T(8,128)(2,1)}, u32[]{:S(2)}) copy-start(bf16[4,8,8,64]{3,2,1,0:T(8,128)(2,1)} %slice.761) | copy-start | bytes 98308
  120.1 11.2 %copy-start.17 = (bf16[4,8,8,64]{3,2,1,0:T(8,128)(2,1)S(1)}, bf16[4,8,8,64]{3,2,1,0:T(8,128)(2,1)}, u32[]{:S(2)}) copy-start(bf16[4,8,8,64]{3,2,1,0:T(8,128)(2,1)} %slice.743) | copy-start | bytes 98308
  123.4 13.0 %copy-start.19 = (bf16[4,8,8,64]{3,2,1,0:T(8,128)(2,1)S(1)}, bf16[4,8,8,64]{3,2,1,0:T(8,128)(2,1)}, u32[]{:S(2)}) copy-start(bf16[4,8,8,64]{3,2,1,0:T(8,128)(2,1)} %slice.752) | copy-start | bytes 98308
  124.2 12.3 %copy-start.15 = (bf16[4,8,8,64]{3,2,1,0:T(8,128)(2,1)S(1)}, bf16[4,8,8,64]{3,2,1,0:T(8,128)(2,1)}, u32[]{:S(2)}) copy-start(bf16[4,8,8,64]{3,2,1,0:T(8,128)(2,1)} %slice.754) | copy-start | bytes 98308
  124.2 12.5 %copy-start.13 = (bf16[4,8,8,64]{3,2,1,0:T(8,128)(2,1)S(1)}, bf16[4,8,8,64]{3,2,1,0:T(8,128)(2,1)}, u32[]{:S(2)}) copy-start(bf16[4,8,8,64]{3,2,1,0:T(8,128)(2,1)} %slice.755) | copy-start | bytes 98308
  124.2 106.4 %all-reduce.7.cloned.1.call-start = ((), (), s32[]{:S(2)}) async-start(), calls=%async_computation.1 | async-start | bytes 1769472 | tf_op jit(solution)/shard_map/psum | solution.py:11
  125.3 11.9 %copy-start.9 = (bf16[4,8,8,64]{3,2,1,0:T(8,128)(2,1)S(1)}, bf16[4,8,8,64]{3,2,1,0:T(8,128)(2,1)}, u32[]{:S(2)}) copy-start(bf16[4,8,8,64]{3,2,1,0:T(8,128)(2,1)} %slice.760) | copy-start | bytes 98308
  126.3 11.8 %copy-start.7 = (bf16[4,8,8,64]{3,2,1,0:T(8,128)(2,1)S(1)}, bf16[4,8,8,64]{3,2,1,0:T(8,128)(2,1)}, u32[]{:S(2)}) copy-start(bf16[4,8,8,64]{3,2,1,0:T(8,128)(2,1)} %slice.761) | copy-start | bytes 98308
  137.2 51.0 %copy-start = (f32[8,16,16,64]{3,2,1,0:T(8,128)S(1)}, f32[8,16,16,64]{3,2,1,0:T(8,128)}, u32[]{:S(2)}) copy-start(f32[8,16,16,64]{3,2,1,0:T(8,128)} %reshape.539) | copy-start | bytes 1572868
  144.3 43.8 %copy-start.26 = (f32[8,16,16]{2,1,0:T(8,128)S(1)}, f32[8,16,16]{2,1,0:T(8,128)}, u32[]{:S(2)}) copy-start(f32[8,16,16]{2,1,0:T(8,128)} %convert_element_type.102) | copy-start | bytes 24580
  146.1 6.5 %collective-permute-start.1 = (bf16[8,1088]{1,0:T(8,128)(2,1)S(1)}, bf16[8,1088]{1,0:T(8,128)(2,1)S(1)}, u32[]{:S(2)}, u32[]{:S(2)}) collective-permute-start(bf16[8,1088]{1,0:T(8,128)(2,1)S(1)} %convert_element_type.109), channel_id=1, source_target_pairs={{16,0},{24,8},{17,1},{25,9},{18,2},{26,10},{19,3},{27,11},{20,4},{... | collective-permute-start | bytes 52232 | tf_op jit(solution)/shard_map/ppermute | solution.py:17
  155.6 28.4 %collective-permute-start.2 = (bf16[8,1024]{1,0:T(8,128)(2,1)S(1)}, bf16[8,1024]{1,0:T(8,128)(2,1)S(1)}, u32[]{:S(2)}, u32[]{:S(2)}) collective-permute-start(bf16[8,1024]{1,0:T(8,128)(2,1)S(1)} %convert_element_type.111), channel_id=1, source_target_pairs={{8,0},{16,8},{24,16},{9,1},{17,9},{25,17},{10,2},{18,10},{26,18},{... | collective-permute-start | bytes 49160 | tf_op jit(solution)/shard_map/ppermute | solution.py:17
Sparse Core Ops, SparseCore 0:
  124.4 57.8 all-reduce.4
  184.7 45.9 all-reduce.6
